TPU v7x, 512 devices: a whole 4x4x16 slice. The times are simulated.
512 devices in a mesh: row: 32 (over x, z_hi, core), col: 16 (over z_lo, y).
Axes of the slice: x: 4, y: 4, z: 16 (z_hi: 4, z_lo: 4; z = z_hi * 4 + z_lo), core: 2. Of those that a mesh axis runs over, the one named last changes fastest.
Arguments:
- images: bfloat16 [32, 128, 128, 256], P('row', 'col'), may hold values from -6 to 6
- weight: bfloat16 [3, 3, 256, 256], P(None, None, None, 'col'), may hold values from -0.125 to 0.125
- norm_gain: float32 [256], replicated, may hold values from 0.5 to 1.5
- cotangent: bfloat16 [32, 128, 128, 256], P('row', 'col'), may hold values from -6 to 6
Outputs:
- features: bfloat16 [32, 128, 128, 256], P('row', 'col')
- input_grad: bfloat16 [32, 128, 128, 256], P('row', 'col')
- weight_grad: float32 [3, 3, 256, 256], P(None, None, None, 'col')
All inputs are finite; a program needn't handle non-finite values.
Results may differ from a plain program's by a relative error of at most 0.013.
Values may be sent and summed in bfloat16 or wider, within the bound.
No kernel may reach another device: no remote copies, remote signals or barrier semaphores. Data moves between devices by JAX's collectives and lax.ppermute only.
A program may use at most 64 MiB of HBM per device.

v0:
```python
import math
import jax
import jax.numpy as jnp
from jax import lax
from jax.sharding import PartitionSpec as P

epsilon = 1e-06
root_half = 0.7071067811865476
norm_const = 0.3989422804014327


def padded_2(value, sides, width):
    for axis, dim in sides:
        peers, length = (lax.axis_size(axis), value.shape[dim])
        up = [(i, (i + 1) % peers) for i in range(peers - 1)]
        down = [(j, i) for i, j in up]
        last = lax.slice_in_dim(value, length - width, length, axis=dim)
        initial = lax.slice_in_dim(value, 0, width, axis=dim)
        before = lax.ppermute(last, axis, up)
        after = lax.ppermute(initial, axis, down)
        value = jnp.concatenate([before, value, after], axis=dim)
    return value


def norm_act(conv_out, upper, norm_gain):
    mean_val = jnp.mean(conv_out, axis=-1, keepdims=True)
    centred = conv_out - mean_val
    variance = jnp.mean(centred * centred, axis=-1, keepdims=True)
    inv_std = lax.rsqrt(variance + epsilon)
    unit = centred * inv_std
    normed = unit * norm_gain
    cdf_val = 0.5 * (1.0 + lax.erf(normed * root_half))
    density = jnp.exp(-0.5 * normed * normed) * norm_const
    outputs = (normed * cdf_val).astype(jnp.bfloat16)
    upstream = upper.astype(jnp.float32) * (cdf_val + normed * density) * norm_gain
    mean_up = jnp.mean(upstream, axis=-1, keepdims=True)
    mean_cross = jnp.mean(upstream * unit, axis=-1, keepdims=True)
    grad_pre = inv_std * (upstream - mean_up - unit * mean_cross)
    return (outputs, grad_pre.astype(jnp.bfloat16))


def window(padded, tap_row, tap_col, tile_rows, tile_cols):
    return padded[:, tap_row : tap_row + tile_rows, tap_col : tap_col + tile_cols, :].reshape(
        -1, padded.shape[-1]
    )


def on_device(images, weight, norm_gain, cotangent):
    img_count, tile_rows, tile_cols, in_chan = images.shape
    whole_kernel = lax.all_gather(weight, "col", axis=3, tiled=True)
    out_chan = whole_kernel.shape[3]
    rimmed = padded_2(images, (("col", 1),), 1)
    padded = jnp.pad(rimmed, ((0, 0), (0, 0), (1, 1), (0, 0)))
    conv_out = jnp.zeros((img_count * tile_rows * tile_cols, out_chan), jnp.float32)
    for tap_row in range(3):
        for tap_col in range(3):
            conv_out = conv_out + jnp.dot(
                window(padded, tap_row, tap_col, tile_rows, tile_cols),
                whole_kernel[tap_row, tap_col],
                preferred_element_type=jnp.float32,
            )
    outputs, grad_pre = norm_act(conv_out, cotangent.reshape(-1, out_chan), norm_gain)
    grad_grid = grad_pre.reshape(img_count, tile_rows, tile_cols, out_chan)
    grad_rimmed = padded_2(grad_grid, (("col", 1),), 1)
    grad_pad = jnp.pad(grad_rimmed, ((0, 0), (0, 0), (1, 1), (0, 0)))
    grad_input = jnp.zeros((img_count * tile_rows * tile_cols, in_chan), jnp.float32)
    pieces = []
    for tap_row in range(3):
        for tap_col in range(3):
            grad_input = grad_input + lax.dot_general(
                window(grad_pad, 2 - tap_row, 2 - tap_col, tile_rows, tile_cols),
                whole_kernel[tap_row, tap_col],
                (((1,), (1,)), ((), ())),
                preferred_element_type=jnp.float32,
            )
            pieces.append(
                lax.dot_general(
                    window(padded, tap_row, tap_col, tile_rows, tile_cols),
                    grad_pre,
                    (((0,), (0,)), ((), ())),
                    preferred_element_type=jnp.float32,
                )
            )
    partial_value = jnp.stack(pieces).reshape(3, 3, in_chan, out_chan)
    totals = lax.psum(partial_value, ("row", "col"))
    col_share = out_chan // lax.axis_size("col")
    own_share = lax.dynamic_slice_in_dim(totals, lax.axis_index("col") * col_share, col_share, 3)
    pixels = img_count * lax.axis_size("row") * tile_rows * lax.axis_size("col") * tile_cols
    weight_grad = own_share * (1.0 / math.sqrt(pixels))
    features = outputs.reshape(img_count, tile_rows, tile_cols, out_chan)
    input_grad = grad_input.astype(jnp.bfloat16).reshape(img_count, tile_rows, tile_cols, in_chan)
    return (features, input_grad, weight_grad)


def solution(mesh):
    placed = (
        P("row", "col", None, None),
        P(None, None, None, "col"),
        P(),
        P("row", "col", None, None),
    )
    return jax.shard_map(
        on_device,
        mesh=mesh,
        in_specs=placed,
        out_specs=(
            P("row", "col", None, None),
            P("row", "col", None, None),
            P(None, None, None, "col"),
        ),
        check_vma=False,
    )
```

profile of v0, /device:TPU:2, one launch (start us, length us, event | category | flops | bytes accessed | tf_op | source)
XLA Modules:
  0.0 616.7 jit_solution(12036107945683514388)
XLA Ops:
  7.2 0.7 all-gather.2.cloned.1.call-update
  8.0 0.9 fusion.29
  8.8 3.5 collective-permute-start
  12.3 1.3 collective-permute-start.1
  13.6 0.6 collective-permute-done
  14.2 4.3 collective-permute-done.1
  18.5 1.2 select_maximum_fusion.2
  19.7 1.0 pad_maximum_fusion.2
  20.8 1.4 fusion.27
  22.1 79.2 %all-gather.2.cloned.1.call-done = bf16[3,3,256,256]{2,3,1,0:T(8,128)(2,1)} async-done(((bf16[3,3,256,16]{2,3,1,0:T(8,128)(2,1)}), bf16[3,3,256,256]{2,3,1,0:T(8,128)(2,1)}) %all-gather.2.cloned.1.call-update) | async-done | bytes 1179664 | tf_op jit(solution)/shard_map/all_gather | solution.py:50
  101.3 1.4 fusion.21
  102.7 0.3 fusion.23
  103.0 0.3 convolution_add_fusion.13
  103.4 0.7 copy-done.6
  104.0 0.3 convolution_add_fusion.12
  104.4 0.3 convolution_add_fusion.11
  104.8 0.3 convolution_add_fusion.10
  105.1 0.7 copy-done.4
  105.8 0.3 convolution_add_fusion.9
  106.2 0.3 convolution_add_fusion.8
  106.5 0.7 copy-done.7
  107.2 0.4 fusion.30
  107.7 0.4 multiply_reduce_fusion.1
  108.1 0.6 copy-done.9
  108.7 1.9 fusion.24
  110.6 0.8 multiply_convert_fusion
  111.5 1.0 fusion.12
  112.5 1.1 fusion.11
  113.5 1.1 fusion.10
  114.6 1.1 fusion.9
  115.7 1.0 fusion.8
  116.7 1.0 fusion.7
  117.8 1.0 fusion.6
  118.8 1.0 fusion.5
  119.8 3.0 collective-permute-start.2
  122.9 1.3 collective-permute-start.3
  124.2 1.0 fusion.4
  125.2 3.1 copy.8
  128.4 0.6 collective-permute-done.3
  129.2 0.4 fusion.26
  129.7 0.3 fusion.20
  130.0 0.3 fusion.22
  130.3 0.3 convolution_add_fusion.6
  130.6 0.3 convolution_add_fusion.5
  131.5 0.3 convolution_add_fusion.2
  132.1 1.1 fusion.3
  133.2 475.1 %all-reduce.4.cloned.1.call-done = f32[3,3,256,256]{2,3,1,0:T(8,128)} async-done(((f32[3,3,256,256]{2,3,1,0:T(8,128)}), f32[3,3,256,256]{2,3,1,0:T(8,128)}) %all-reduce.4.cloned.1.call-update) | async-done | bytes 2359312 | tf_op jit(solution)/shard_map/psum | solution.py:85
  608.3 1.6 dynamic-slice_multiply_fusion
  (31 shorter events, 1.4 us)
Async XLA Ops:
  7.2 12.6 %copy-start = (bf16[1,8,128,256]{3,2,1,0:T(8,128)(2,1)S(1)}, bf16[1,8,128,256]{3,2,1,0:T(8,128)(2,1)}, u32[]{:S(2)}) copy-start(bf16[1,8,128,256]{3,2,1,0:T(8,128)(2,1)} %param.4) | copy-start | bytes 1572868
  7.2 94.1 %all-gather.2.cloned.1.call-start = ((), (), s32[]{:S(2)}) async-start(), calls=%async_computation | async-start | bytes 1253376 | tf_op jit(solution)/shard_map/all_gather | solution.py:50
  7.9 600.3 %all-reduce.4.cloned.1.call-start = ((), (), s32[]{:S(2)}) async-start(), calls=%async_computation.1 | async-start | bytes 4718592 | tf_op jit(solution)/shard_map/psum | solution.py:85
  8.8 5.4 collective-permute-start
  12.3 6.2 collective-permute-start.1
  22.1 84.1 %copy-start.2 = (bf16[1,8,128,256]{3,2,1,0:T(8,128)(2,1)}, bf16[1,8,128,256]{3,2,1,0:T(8,128)(2,1)S(1)}, u32[]{:S(2)}) copy-start(bf16[1,8,128,256]{3,2,1,0:T(8,128)(2,1)S(1)} %get-tuple-element.13) | copy-start | bytes 1572868
  101.3 1.4 copy-start.1
  101.3 1.7 copy-start.8
  103.0 1.0 copy-start.6
  103.4 1.1 copy-start.5
  104.8 1.0 copy-start.4
  106.2 1.0 copy-start.7
  107.2 0.8 copy-start.10
  107.6 1.0 copy-start.9
  115.7 2.1 copy-start.3
  119.8 8.6 %collective-permute-start.2 = (bf16[1,1,128,256]{3,2,1,0:T(8,128)(2,1)S(1)}, bf16[1,1,128,256]{3,2,1,0:T(8,128)(2,1)S(1)}, u32[]{:S(2)}, u32[]{:S(2)}) collective-permute-start(bf16[1,1,128,256]{3,2,1,0:T(8,128)(2,1)S(1)} %get-tuple-element.21), channel_id=1, source_target_pairs={{0,1},{1,2},{2,3},{3,4},{4,5},{5,6},{6,7},{7,8},{8,9},{9,10},{10,1... | collective-permute-start | bytes 196616 | tf_op jit(solution)/shard_map/ppermute | solution.py:19
  122.9 6.2 collective-permute-start.3
Sparse Core Ops, SparseCore 0:
  10.1 91.1 all-gather.1
  128.5 479.7 all-reduce.3
where the time goes:
time: 617 us
  waiting for transfers between devices  560 us (91%)
  matrix products  17 us (3%)
  between operations  14.3 us (2%)
  starting transfers between devices  9.17 us (1%)
  local copies, waits for them, and re-layouts  8.58 us (1%)
  other arithmetic  7.21 us (1%)
    psum x1, waiting for transfers between devices, on_device(): totals = lax.psum(partial_value, ('row', 'col'))  475 us
    all_gather x1, waiting for transfers between devices, on_device(): whole_kernel = lax.all_gather(weight, 'col', axis=3, tiled=True)  79.2 us
  transfers between devices with their start and end apart: 6, of which 5 were waited for; matrix products, arithmetic and copies ran while one was open for 2% of the time, Pallas kernels for 0%

commit v1 on v0

--- a/solution.py
+++ b/solution.py
@@ -82,7 +82,7 @@
                 )
             )
     partial_value = jnp.stack(pieces).reshape(3, 3, in_chan, out_chan)
-    totals = lax.psum(partial_value, ("row", "col"))
+    totals = lax.psum(lax.psum(partial_value, "row"), "col")
     col_share = out_chan // lax.axis_size("col")
     own_share = lax.dynamic_slice_in_dim(totals, lax.axis_index("col") * col_share, col_share, 3)
     pixels = img_count * lax.axis_size("row") * tile_rows * lax.axis_size("col") * tile_cols

time: 617 us -> 664 us (1.076)
  waiting for transfers between devices: 560 us -> 605 us
    psum x1 -> x2, waiting for transfers between devices: 475 us -> 515 us  [on_device(): totals = lax.psum(lax.psum(partial_value, 'row'), 'col')]
  transfers between devices with their start and end apart: 6 -> 7, of which waited for: 5 -> 7; matrix products, arithmetic and copies ran while one was open for 2% -> 1% of each run, Pallas kernels for 0% -> 0%
where the time goes in v1:
time: 664 us
  waiting for transfers between devices  605 us (91%)
  matrix products  16.9 us (3%)
  between operations  14.1 us (2%)
  local copies, waits for them, and re-layouts  11.2 us (2%)
  starting transfers between devices  9.21 us (1%)
  other arithmetic  7.23 us (1%)
    psum x2, waiting for transfers between devices, on_device(): totals = lax.psum(lax.psum(partial_value, 'row'), 'col')  515 us
    all_gather x1, waiting for transfers between devices, on_device(): whole_kernel = lax.all_gather(weight, 'col', axis=3, tiled=True)  79.2 us
  transfers between devices with their start and end apart: 7, of which 7 were waited for; matrix products, arithmetic and copies ran while one was open for 1% of the time, Pallas kernels for 0%

profile of v1, /device:TPU:2, one launch (start us, length us, event | category | flops | bytes accessed | tf_op | source)
XLA Modules:
  0.0 663.7 jit_solution(10248189167685522920)
XLA Ops:
  7.2 0.7 all-gather.2.cloned.1.call-update
  8.0 0.9 fusion.29
  8.8 3.5 collective-permute-start
  12.3 1.3 collective-permute-start.1
  13.6 0.6 collective-permute-done
  14.2 4.3 collective-permute-done.1
  18.5 1.2 select_maximum_fusion.2
  19.7 1.0 pad_maximum_fusion.2
  20.8 1.4 fusion.27
  22.1 79.2 %all-gather.2.cloned.1.call-done = bf16[3,3,256,256]{2,3,1,0:T(8,128)(2,1)} async-done(((bf16[3,3,256,16]{2,3,1,0:T(8,128)(2,1)}), bf16[3,3,256,256]{2,3,1,0:T(8,128)(2,1)}) %all-gather.2.cloned.1.call-update) | async-done | bytes 1179664 | tf_op jit(solution)/shard_map/all_gather | solution.py:50
  101.3 1.4 fusion.21
  102.7 0.3 fusion.23
  103.0 0.3 convolution_add_fusion.13
  103.4 0.7 copy-done.6
  104.0 0.3 convolution_add_fusion.12
  104.4 0.3 convolution_add_fusion.11
  104.8 0.3 convolution_add_fusion.10
  105.1 0.7 copy-done.4
  105.8 0.3 convolution_add_fusion.9
  106.2 0.3 convolution_add_fusion.8
  106.5 0.7 copy-done.11
  107.2 0.4 fusion.30
  107.7 0.4 multiply_reduce_fusion.1
  108.1 0.6 copy-done.13
  108.7 1.9 fusion.24
  110.6 0.8 multiply_convert_fusion
  111.5 1.0 fusion.12
  112.5 1.0 fusion.11
  113.5 1.0 fusion.10
  114.5 1.0 fusion.9
  115.6 1.1 fusion.8
  116.7 1.0 fusion.7
  117.7 1.0 fusion.6
  118.7 1.1 fusion.5
  119.8 1.0 fusion.4
  120.8 3.0 copy.8
  124.0 3.0 collective-permute-start.2
  127.0 1.3 collective-permute-start.3
  128.3 0.6 collective-permute-done.2
  128.9 4.3 collective-permute-done.3
  133.3 1.6 fusion.26
  135.2 329.7 %all-reduce.5.cloned.1.call-done = f32[3,3,256,256]{2,3,1,0:T(8,128)} async-done(((f32[3,3,256,256]{2,3,1,0:T(8,128)}), f32[3,3,256,256]{2,3,1,0:T(8,128)}) %all-reduce.5.cloned.1.call-update) | async-done | bytes 2359312 | tf_op jit(solution)/shard_map/psum | solution.py:85
  465.6 0.7 copy-done.10
  467.0 0.3 convolution_add_fusion.3
  467.3 0.7 copy-done.8
  468.7 1.1 fusion.3
  469.8 185.8 %all-reduce.7.cloned.1.call-done = f32[3,3,256,256]{2,3,1,0:T(8,128)} async-done(((f32[3,3,256,256]{2,3,1,0:T(8,128)}), f32[3,3,256,256]{2,3,1,0:T(8,128)}) %all-reduce.7.cloned.1.call-update) | async-done | bytes 2359312 | tf_op jit(solution)/shard_map/psum | solution.py:85
  655.6 1.6 dynamic-slice_multiply_fusion
  (42 shorter events, 2.7 us)
Async XLA Ops:
  7.2 12.6 %copy-start = (bf16[1,8,128,256]{3,2,1,0:T(8,128)(2,1)S(1)}, bf16[1,8,128,256]{3,2,1,0:T(8,128)(2,1)}, u32[]{:S(2)}) copy-start(bf16[1,8,128,256]{3,2,1,0:T(8,128)(2,1)} %param.4) | copy-start | bytes 1572868
  7.2 94.1 %all-gather.2.cloned.1.call-start = ((), (), s32[]{:S(2)}) async-start(), calls=%async_computation | async-start | bytes 1253376 | tf_op jit(solution)/shard_map/all_gather | solution.py:50
  7.9 457.0 %all-reduce.5.cloned.1.call-start = ((), (), s32[]{:S(2)}) async-start(), calls=%async_computation.1 | async-start | bytes 4718592 | tf_op jit(solution)/shard_map/psum | solution.py:85
  8.8 5.4 collective-permute-start
  12.3 6.2 collective-permute-start.1
  22.1 84.0 %copy-start.2 = (bf16[1,8,128,256]{3,2,1,0:T(8,128)(2,1)}, bf16[1,8,128,256]{3,2,1,0:T(8,128)(2,1)S(1)}, u32[]{:S(2)}) copy-start(bf16[1,8,128,256]{3,2,1,0:T(8,128)(2,1)S(1)} %get-tuple-element.13) | copy-start | bytes 1572868
  101.3 1.4 copy-start.1
  101.3 1.7 copy-start.12
  103.0 1.0 copy-start.6
  103.4 1.1 copy-start.5
  104.8 1.0 copy-start.4
  106.2 1.0 copy-start.11
  107.2 0.8 copy-start.14
  107.6 1.0 copy-start.13
  115.6 2.1 copy-start.3
  123.9 531.7 %all-reduce.7.cloned.1.call-start = ((), (), s32[]{:S(2)}) async-start(), calls=%async_computation.2 | async-start | bytes 4718592 | tf_op jit(solution)/shard_map/psum | solution.py:85
  124.0 4.9 collective-permute-start.2
  127.0 6.2 collective-permute-start.3
  465.3 1.0 copy-start.10
  465.6 1.1 copy-start.9
  467.0 1.0 copy-start.8
  467.3 1.1 copy-start.7
Sparse Core Ops, SparseCore 0:
  10.1 91.1 all-gather.1
  124.0 340.8 all-reduce.4
  467.8 187.6 all-reduce.6
